TPU v7x, 512 devices: a whole 4x8x8 slice. The times are simulated.
512 devices in a mesh: expert: 64 (over x, z, core), group: 8 (over y).
Axes of the slice: x: 4, y: 8, z: 8, core: 2. Of those that a mesh axis runs over, the one named last changes fastest.
Arguments:
- tokens: bfloat16 [4096, 4096], P('expert', 'group'), may hold values from -6 to 6
- gate_weight: bfloat16 [64, 1536, 4096], P('expert', 'group'), may hold values from -0.09375 to 0.09375
- up_weight: bfloat16 [64, 1536, 4096], P('expert', 'group'), may hold values from -0.09375 to 0.09375
- down_weight: bfloat16 [64, 1536, 4096], P('expert', 'group'), may hold values from -0.15625 to 0.15625
- expert_ids: int32 [4096, 8], P('expert'), may hold values from 0 to 63, all different within a row; in each aligned block of 64 rows (0 to 63, 64 to 127, ...) at most 12 rows name the same one
- gate_scores: bfloat16 [4096, 8], P('expert'), may hold values from 0.19921875 to 1
Outputs:
- mixed: bfloat16 [4096, 4096], P('expert', 'group')
Inputs may be any that keep to these rules, and one draw needn't show every extreme that they name: `expert_ids`: the 8 experts of a token are distinct; within the 64 rows of one device no expert is named by more than 12 rows, a bound that some block reaches.
All inputs are finite; a program needn't handle non-finite values.
Results may differ from a plain program's by a relative error of at most 0.019.
Values may be sent and summed in bfloat16 or wider, within the bound.
No kernel may reach another device: no remote copies, remote signals or barrier semaphores. Data moves between devices by JAX's collectives and lax.ppermute only.
A program may use at most 128 MiB of HBM per device.

v0:
```python
import jax
import jax.numpy as jnp
from jax import lax
from jax.sharding import PartitionSpec as P


def route_tables(expert_ids, gate_scores, experts):
    tok_rows, top_count = expert_ids.shape
    capacity = tok_rows * top_count * 3 // (2 * experts)
    flat_ids = expert_ids.reshape(-1)
    onehot = (flat_ids[:, None] == jnp.arange(experts, dtype=jnp.int32)[None, :]).astype(jnp.int32)
    before = jnp.cumsum(onehot, axis=0) - onehot
    slot_index = jnp.sum(before * onehot, axis=1).reshape(tok_rows, top_count)
    slot_keys = expert_ids * capacity + slot_index
    columns = jnp.arange(experts * capacity, dtype=jnp.int32)
    matches = slot_keys[:, :, None] == columns[None, None, :]
    selector = jnp.any(matches, axis=1).astype(jnp.bfloat16)
    weights = jnp.sum(
        jnp.where(matches, gate_scores[:, :, None].astype(jnp.float32), 0.0), axis=1
    ).astype(jnp.bfloat16)
    return (capacity, selector, weights)


def per_device(tokens, gate_weight, up_weight, down_weight, expert_ids, gate_scores):
    experts = lax.axis_size("expert")
    capacity, selector, weights = route_tables(expert_ids, gate_scores, experts)
    placed = lax.dot_general(
        selector, tokens, (((0,), (0,)), ((), ())), preferred_element_type=jnp.float32
    ).astype(jnp.bfloat16)
    arrived = lax.all_to_all(
        placed.reshape(experts, capacity, tokens.shape[1]), "expert", 0, 0, tiled=True
    ).reshape(experts * capacity, tokens.shape[1])
    row_block = lax.all_gather(arrived, "group", axis=1, tiled=True)
    gate_value = lax.dot_general(
        row_block, gate_weight[0], (((1,), (1,)), ((), ())), preferred_element_type=jnp.float32
    )
    up_value = lax.dot_general(
        row_block, up_weight[0], (((1,), (1,)), ((), ())), preferred_element_type=jnp.float32
    )
    hidden = (jax.nn.silu(gate_value) * up_value).astype(jnp.bfloat16)
    hidden_all = lax.all_gather(hidden, "group", axis=1, tiled=True)
    down_cols = lax.all_to_all(down_weight[0], "group", 1, 0, tiled=True)
    partial_value = jnp.dot(hidden_all, down_cols, preferred_element_type=jnp.float32)
    returned = lax.all_to_all(
        partial_value.astype(jnp.bfloat16).reshape(experts, capacity, -1),
        "expert",
        0,
        0,
        tiled=True,
    ).reshape(experts * capacity, -1)
    combined = jnp.dot(weights, returned, preferred_element_type=jnp.float32)
    return combined.astype(jnp.bfloat16)


def solution(mesh):
    placed = (
        P("expert", "group"),
        P("expert", "group", None),
        P("expert", "group", None),
        P("expert", "group", None),
        P("expert", None),
        P("expert", None),
    )
    return jax.shard_map(
        per_device, mesh=mesh, in_specs=placed, out_specs=P("expert", "group"), check_vma=False
    )
```

profile of v0, /device:TPU:1, one launch (start us, length us, event | category | flops | bytes accessed | tf_op | source)
XLA Modules:
  0.0 261.2 jit_solution(7376772480139769284)
XLA Ops:
  6.5 0.9 copy.36
  7.6 1.2 reduce-window.6
  8.8 0.2 slice_reduce_fusion
  9.1 0.1 fusion.13
  9.4 0.7 multiply_add_fusion
  10.2 0.5 fusion.4
  10.7 1.3 convolution_convert_fusion
  12.0 0.2 reshape.41
  12.2 43.3 %all_to_all.29 = bf16[64,12,512]{2,1,0:T(8,128)(2,1)} all-to-all(bf16[64,12,512]{2,1,0:T(8,128)(2,1)S(1)} %reshape.41), channel_id=1, replica_groups=mesh['expert'=64,'group'=8] {'expert'}, dimensions={0} | all-to-all | bytes 1572864 | tf_op jit(solution)/shard_map/all_to_all | solution.py:30
  55.4 2.1 reshape.42
  57.6 73.5 %all-gather.3.cloned.1.call-done = bf16[768,4096]{1,0:T(8,128)(2,1)} async-done(((bf16[768,512]{1,0:T(8,128)(2,1)}), bf16[768,4096]{1,0:T(8,128)(2,1)}) %all-gather.3.cloned.1.call-update) | async-done | bytes 6291472 | tf_op jit(solution)/shard_map/all_gather | solution.py:33
  131.1 5.2 %fusion.2 = f32[768,192]{0,1:T(8,128)S(1)} fusion(bf16[768,4096]{1,0:T(8,128)(2,1)} %all-gather.3.cloned.1.call-done, bf16[1,192,4096]{2,1,0:T(8,128)(2,1)S(1)} %copy-done), kind=kOutput, calls=%fused_computation.2 | convolution fusion | flops 1207959552 | bytes 8454144 | tf_op jit(solution)/shard_map/dot_general | solution.py:34
  136.3 4.5 %fusion.8 = bf16[768,192]{0,1:T(8,128)(2,1)} fusion(bf16[768,4096]{1,0:T(8,128)(2,1)S(1)} %copy-done.3, bf16[1,192,4096]{2,1,0:T(8,128)(2,1)} %param.8, f32[768,192]{0,1:T(8,128)S(1)} %fusion.2), kind=kOutput, calls=%fused_computation.10 | convolution fusion | flops 1208844288 | bytes 8749056 | tf_op jit(solution)/shard_map/dot_general | solution.py:37
  140.8 0.6 copy.44
  141.5 0.5 copy.42
  142.0 55.0 %all_to_all.30 = bf16[192,8,512]{2,0,1:T(8,128)(2,1)S(1)} all-to-all(bf16[192,8,512]{2,0,1:T(8,128)(2,1)S(1)} %copy.42), channel_id=1, replica_groups=mesh['expert'=64,'group'=8] {'group'}, dimensions={1} | all-to-all | bytes 3145728 | tf_op jit(solution)/shard_map/all_to_all | solution.py:42
  197.0 9.2 %all-gather.5.cloned.1.call-done = bf16[768,1536]{0,1:T(8,128)(2,1)} async-done(((bf16[768,192]{0,1:T(8,128)(2,1)}), bf16[768,1536]{0,1:T(8,128)(2,1)}) %all-gather.5.cloned.1.call-update) | async-done | bytes 2359312 | tf_op jit(solution)/shard_map/all_gather | solution.py:41
  206.2 4.0 %convolution_convert_fusion.1 = bf16[768,512]{1,0:T(8,128)(2,1)} fusion(bf16[768,1536]{0,1:T(8,128)(2,1)} %all-gather.5.cloned.1.call-done, bf16[1536,512]{1,0:T(8,128)(2,1)S(1)} %bitcast.45), kind=kOutput, calls=%fused_computation.8 | convolution fusion | flops 1208352768 | bytes 4718592 | tf_op jit(solution)/shard_map/dot_general | solution.py:43
  210.2 2.1 reshape.43
  212.3 12.4 %all-to-all-start.2 = ((bf16[64,12,512]{2,1,0:T(8,128)(2,1)}), bf16[64,12,512]{2,1,0:T(8,128)(2,1)S(1)}, u32[]{:S(2)}, u32[]{:S(2)}) async-start(bf16[64,12,512]{2,1,0:T(8,128)(2,1)} %reshape.43), calls=%async_computation.2 | async-start | bytes 2097152 | tf_op jit(solution)/shard_map/all_to_all | solution.py:44
  224.8 0.6 select_reduce_fusion
  225.4 27.9 %all-to-all-done.2 = bf16[64,12,512]{2,1,0:T(8,128)(2,1)S(1)} async-done(((bf16[64,12,512]{2,1,0:T(8,128)(2,1)}), bf16[64,12,512]{2,1,0:T(8,128)(2,1)S(1)}, u32[]{:S(2)}, u32[]{:S(2)}) %all-to-all-start.2) | async-done | bytes 786464 | tf_op jit(solution)/shard_map/all_to_all | solution.py:44
  253.3 0.2 reshape.44
  253.4 0.9 convolution_convert_fusion.2
  (21 shorter events, 0.7 us)
Async XLA Ops:
  6.5 124.6 %copy-start = (bf16[1,192,4096]{2,1,0:T(8,128)(2,1)S(1)}, bf16[1,192,4096]{2,1,0:T(8,128)(2,1)}, u32[]{:S(2)}) copy-start(bf16[1,192,4096]{2,1,0:T(8,128)(2,1)} %param.7) | copy-start | bytes 4718596
  6.5 124.6 %all-gather.3.cloned.1.call-start = ((), (), s32[]{:S(2)}) async-start(), calls=%async_computation.3 | async-start | bytes 7077888 | tf_op jit(solution)/shard_map/all_gather | solution.py:33
  57.5 148.7 %all-gather.5.cloned.1.call-start = ((), (), s32[]{:S(2)}) async-start(), calls=%async_computation.4 | async-start | bytes 2654208 | tf_op jit(solution)/shard_map/all_gather | solution.py:41
  131.1 5.2 %copy-start.3 = (bf16[768,4096]{1,0:T(8,128)(2,1)S(1)}, bf16[768,4096]{1,0:T(8,128)(2,1)}, u32[]{:S(2)}) copy-start(bf16[768,4096]{1,0:T(8,128)(2,1)} %all-gather.3.cloned.1.call-done) | copy-start | bytes 18874372
  136.3 4.5 %copy-start.1 = (bf16[1,192,4096]{2,1,0:T(8,128)(2,1)S(1)}, bf16[1,192,4096]{2,1,0:T(8,128)(2,1)}, u32[]{:S(2)}) copy-start(bf16[1,192,4096]{2,1,0:T(8,128)(2,1)} %param.9) | copy-start | bytes 4718596
  210.2 14.6 %copy-start.2 = (bf16[64,8]{0,1:T(8,128)(2,1)S(1)}, bf16[64,8]{0,1:T(8,128)(2,1)}, u32[]{:S(2)}) copy-start(bf16[64,8]{0,1:T(8,128)(2,1)} %param.11) | copy-start | bytes 3076
  212.3 41.0 %all-to-all-start.2 = ((bf16[64,12,512]{2,1,0:T(8,128)(2,1)}), bf16[64,12,512]{2,1,0:T(8,128)(2,1)S(1)}, u32[]{:S(2)}, u32[]{:S(2)}) async-start(bf16[64,12,512]{2,1,0:T(8,128)(2,1)} %reshape.43), calls=%async_computation.2 | async-start | bytes 2097152 | tf_op jit(solution)/shard_map/all_to_all | solution.py:44
Sparse Core Ops, SparseCore 0:
  57.7 73.4 all-gather.2
  140.9 65.2 all-gather.4
where the time goes:
time: 262 us; the launch traced here: 261 us
  waiting for transfers between devices  111 us (42%)
  blocking collectives  98.3 us (38%)
  matrix products  15.8 us (6%)
  between operations  13.5 us (5%)
  starting transfers between devices  12.5 us (5%)
  local copies, waits for them, and re-layouts  7.35 us (3%)
  other arithmetic  3.17 us (1%)
    all_gather x1, waiting for transfers between devices, per_device(): row_block = lax.all_gather(arrived, 'group', axis=1, tiled=True)  73.5 us
    all_to_all x1, blocking collectives, per_device(): down_cols = lax.all_to_all(down_weight[0], 'group', 1, 0, tiled=True)  55 us
    all_to_all x1, blocking collectives, per_device(): lax.all_to_all(placed.reshape(experts, capacity, tokens.shape[1]), 'exper...  43.3 us
    all_to_all x1, waiting for transfers between devices, per_device(): lax.all_to_all(partial_value.astype(jnp.bfloat16).reshape(experts, capaci...  27.9 us
    all_to_all x1, starting transfers between devices, per_device(): lax.all_to_all(partial_value.astype(jnp.bfloat16).reshape(experts, capaci...  12.4 us
    all_gather x1, waiting for transfers between devices, per_device(): hidden_all = lax.all_gather(hidden, 'group', axis=1, tiled=True)  9.22 us
  transfers between devices with their start and end apart: 3, of which 3 were waited for; matrix products, arithmetic and copies ran while one was open for 1% of the time, Pallas kernels for 0%

commit v1 on v0

--- a/solution.py
+++ b/solution.py
@@ -1,7 +1,17 @@
+import functools
 import jax
 import jax.numpy as jnp
 from jax import lax
 from jax.sharding import PartitionSpec as P
+
+
+def find_rows(chunk, shard_axis):
+    small = jnp.stack(lax.axis_size(shard_axis) * [chunk], axis=0)
+    seen_now = jnp.concatenate(lax.all_to_all(small, shard_axis, 0, 0), 1)
+    return seen_now
+
+
+_move_block = functools.partial(find_rows, shard_axis="group")
 
 
 def route_tables(expert_ids, gate_scores, experts):
@@ -38,7 +48,7 @@
         row_block, up_weight[0], (((1,), (1,)), ((), ())), preferred_element_type=jnp.float32
     )
     hidden = (jax.nn.silu(gate_value) * up_value).astype(jnp.bfloat16)
-    hidden_all = lax.all_gather(hidden, "group", axis=1, tiled=True)
+    hidden_all = _move_block(hidden)
     down_cols = lax.all_to_all(down_weight[0], "group", 1, 0, tiled=True)
     partial_value = jnp.dot(hidden_all, down_cols, preferred_element_type=jnp.float32)
     returned = lax.all_to_all(

time: 262 us -> 281 us (1.073)
  waiting for transfers between devices: 111 us -> 125 us
  blocking collectives: 98.3 us -> 103 us
  matrix products: 15.8 us -> 11.9 us
    all_gather x1, waiting for transfers between devices: 73.5 us -> 97.3 us  [per_device(): row_block = lax.all_gather(arrived, 'group', axis=1, tiled=True)]
    all_gather x1 -> x0, waiting for transfers between devices: 9.22 us -> none  [per_device(): hidden_all = lax.all_gather(hidden, 'group', axis=1, tiled=True)]
    all_to_all x0 -> x1, starting transfers between devices: none -> 6.82 us  [per_device(): down_cols = lax.all_to_all(down_weight[0], 'group', 1, 0, tiled=True)]
    all_to_all x1, blocking collectives: 55 us -> 59.7 us  [find_rows(): seen_now = jnp.concatenate(lax.all_to_all(small, shard_axis, 0, 0), 1)]
    all_to_all x1, starting transfers between devices: 12.4 us -> 7.72 us  [per_device(): lax.all_to_all(partial_value.astype(jnp.bfloat16).reshape(experts, capaci...]
  transfers between devices with their start and end apart: 3 -> 3, of which waited for: 3 -> 2; matrix products, arithmetic and copies ran while one was open for 1% -> 4% of each run, Pallas kernels for 0% -> 0%
where the time goes in v1:
time: 281 us; the launch traced here: 280 us
  waiting for transfers between devices  125 us (44%)
  blocking collectives  103 us (37%)
  starting transfers between devices  14.5 us (5%)
  between operations  13.5 us (5%)
  matrix products  11.9 us (4%)
  local copies, waits for them, and re-layouts  8.82 us (3%)
  other arithmetic  3.17 us (1%)
    all_gather x1, waiting for transfers between devices, per_device(): row_block = lax.all_gather(arrived, 'group', axis=1, tiled=True)  97.3 us
    all_to_all x1, blocking collectives, find_rows(): seen_now = jnp.concatenate(lax.all_to_all(small, shard_axis, 0, 0), 1)  59.7 us
    all_to_all x1, blocking collectives, per_device(): lax.all_to_all(placed.reshape(experts, capacity, tokens.shape[1]), 'exper...  43.3 us
    all_to_all x1, waiting for transfers between devices, per_device(): lax.all_to_all(partial_value.astype(jnp.bfloat16).reshape(experts, capaci...  27.9 us
    all_to_all x1, starting transfers between devices, per_device(): lax.all_to_all(partial_value.astype(jnp.bfloat16).reshape(experts, capaci...  7.72 us
    all_to_all x1, starting transfers between devices, per_device(): down_cols = lax.all_to_all(down_weight[0], 'group', 1, 0, tiled=True)  6.82 us
  transfers between devices with their start and end apart: 3, of which 2 were waited for; matrix products, arithmetic and copies ran while one was open for 4% of the time, Pallas kernels for 0%

profile of v1, /device:TPU:1, one launch (start us, length us, event | category | flops | bytes accessed | tf_op | source)
XLA Modules:
  0.0 280.1 jit_solution(8050337429065673999)
XLA Ops:
  6.5 0.9 copy.23
  7.6 1.2 reduce-window.6
  8.8 0.2 slice_reduce_fusion
  9.4 0.7 multiply_add_fusion
  10.2 0.5 fusion.7
  10.7 1.3 convolution_convert_fusion
  12.0 0.2 reshape.47
  12.2 43.3 %all_to_all.31 = bf16[64,12,512]{2,1,0:T(8,128)(2,1)} all-to-all(bf16[64,12,512]{2,1,0:T(8,128)(2,1)S(1)} %reshape.47), channel_id=1, replica_groups=mesh['expert'=64,'group'=8] {'expert'}, dimensions={0} | all-to-all | bytes 1572864 | tf_op jit(solution)/shard_map/all_to_all | solution.py:40
  55.4 2.2 reshape.48
  57.7 0.6 copy.31
  58.4 1.6 copy.29
  60.0 6.8 %all-to-all-start.2 = ((bf16[192,8,512]{2,0,1:T(8,128)(2,1)}), bf16[192,8,512]{2,0,1:T(8,128)(2,1)S(1)}, u32[]{:S(2)}, u32[]{:S(2)}) async-start(bf16[192,8,512]{2,0,1:T(8,128)(2,1)} %copy.29), calls=%async_computation.2 | async-start | bytes 3145728 | tf_op jit(solution)/shard_map/all_to_all | solution.py:52
  66.8 97.3 %all-gather.2.cloned.1.call-done = bf16[768,4096]{1,0:T(8,128)(2,1)} async-done(((bf16[768,512]{1,0:T(8,128)(2,1)}), bf16[768,4096]{1,0:T(8,128)(2,1)}) %all-gather.2.cloned.1.call-update) | async-done | bytes 6291472 | tf_op jit(solution)/shard_map/all_gather | solution.py:43
  164.1 5.1 %fusion.5 = f32[768,192]{0,1:T(8,128)S(1)} fusion(bf16[768,4096]{1,0:T(8,128)(2,1)} %all-gather.2.cloned.1.call-done, bf16[1,192,4096]{2,1,0:T(8,128)(2,1)S(1)} %copy-done), kind=kOutput, calls=%fused_computation.6 | convolution fusion | flops 1207959552 | bytes 8454144 | tf_op jit(solution)/shard_map/dot_general | solution.py:44
  169.3 2.2 fusion.15
  171.6 0.2 stack.2
  171.7 59.7 %all_to_all.32 = bf16[8,768,192]{1,2,0:T(8,128)(2,1)S(1)} all-to-all(bf16[8,768,192]{1,2,0:T(8,128)(2,1)S(1)} %stack.2), channel_id=1, replica_groups=mesh['expert'=64,'group'=8] {'group'}, dimensions={0} | all-to-all | bytes 4718592 | tf_op jit(solution)/shard_map/all_to_all | solution.py:10
  231.5 2.3 bitcast_convert_fusion
  233.8 2.1 reshape.50
  235.9 7.7 %all-to-all-start.3 = ((bf16[64,12,512]{2,1,0:T(8,128)(2,1)}), bf16[64,12,512]{2,1,0:T(8,128)(2,1)S(1)}, u32[]{:S(2)}, u32[]{:S(2)}) async-start(bf16[64,12,512]{2,1,0:T(8,128)(2,1)} %reshape.50), calls=%async_computation.3 | async-start | bytes 2097152 | tf_op jit(solution)/shard_map/all_to_all | solution.py:54
  243.8 0.6 select_reduce_fusion
  244.3 27.9 %all-to-all-done.3 = bf16[64,12,512]{2,1,0:T(8,128)(2,1)S(1)} async-done(((bf16[64,12,512]{2,1,0:T(8,128)(2,1)}), bf16[64,12,512]{2,1,0:T(8,128)(2,1)S(1)}, u32[]{:S(2)}, u32[]{:S(2)}) %all-to-all-start.3) | async-done | bytes 786464 | tf_op jit(solution)/shard_map/all_to_all | solution.py:54
  272.2 0.2 reshape.51
  272.4 0.9 convolution_convert_fusion.1
  (23 shorter events, 0.7 us)
Async XLA Ops:
  6.5 157.6 %copy-start = (bf16[1,192,4096]{2,1,0:T(8,128)(2,1)S(1)}, bf16[1,192,4096]{2,1,0:T(8,128)(2,1)}, u32[]{:S(2)}) copy-start(bf16[1,192,4096]{2,1,0:T(8,128)(2,1)} %param.7) | copy-start | bytes 4718596
  6.5 157.6 %all-gather.2.cloned.1.call-start = ((), (), s32[]{:S(2)}) async-start(), calls=%async_computation.4 | async-start | bytes 7077888 | tf_op jit(solution)/shard_map/all_gather | solution.py:43
  55.4 2.3 copy-start.1
  60.0 111.6 %all-to-all-start.2 = ((bf16[192,8,512]{2,0,1:T(8,128)(2,1)}), bf16[192,8,512]{2,0,1:T(8,128)(2,1)S(1)}, u32[]{:S(2)}, u32[]{:S(2)}) async-start(bf16[192,8,512]{2,0,1:T(8,128)(2,1)} %copy.29), calls=%async_computation.2 | async-start | bytes 3145728 | tf_op jit(solution)/shard_map/all_to_all | solution.py:52
  164.1 5.2 %copy-start.3 = (bf16[768,4096]{1,0:T(8,128)(2,1)S(1)}, bf16[768,4096]{1,0:T(8,128)(2,1)}, u32[]{:S(2)}) copy-start(bf16[768,4096]{1,0:T(8,128)(2,1)} %all-gather.2.cloned.1.call-done) | copy-start | bytes 18874372
  164.1 5.2 %copy-start.4 = (bf16[1,192,4096]{2,1,0:T(8,128)(2,1)S(1)}, bf16[1,192,4096]{2,1,0:T(8,128)(2,1)}, u32[]{:S(2)}) copy-start(bf16[1,192,4096]{2,1,0:T(8,128)(2,1)} %param.8) | copy-start | bytes 4718596
  233.8 9.9 %copy-start.2 = (bf16[64,8]{0,1:T(8,128)(2,1)S(1)}, bf16[64,8]{0,1:T(8,128)(2,1)}, u32[]{:S(2)}) copy-start(bf16[64,8]{0,1:T(8,128)(2,1)} %param.11) | copy-start | bytes 3076
  235.9 36.3 %all-to-all-start.3 = ((bf16[64,12,512]{2,1,0:T(8,128)(2,1)}), bf16[64,12,512]{2,1,0:T(8,128)(2,1)S(1)}, u32[]{:S(2)}, u32[]{:S(2)}) async-start(bf16[64,12,512]{2,1,0:T(8,128)(2,1)} %reshape.50), calls=%async_computation.3 | async-start | bytes 2097152 | tf_op jit(solution)/shard_map/all_to_all | solution.py:54
Sparse Core Ops, SparseCore 0:
  57.8 106.2 all-gather.1
